TPU v7x, 128 devices: a whole 4x4x4 slice. The times are simulated.
128 devices in a mesh: seq: 4 (over x), exp: 32 (over y, z, core).
Axes of the slice: x: 4, y: 4, z: 4, core: 2. Of those that a mesh axis runs over, the one named last changes fastest.
Arguments:
- resid: bfloat16 [32, 384, 2048], P('exp', 'seq'), may hold values from -6 to 6
- qkv: bfloat16 [32, 384, 6144], P('exp', 'seq'), may hold values from -8 to 8
- w_out: bfloat16 [2048, 2048], P('seq'), may hold values from -0.125 to 0.125
- norm_gain: float32 [2048], replicated, may hold values from 0.1 to 1.9
- router_w: bfloat16 [2048, 64], replicated, may hold values from -0.125 to 0.125
- expert_ids: int32 [32, 384, 6], P('exp'), may hold values from 0 to 63, all different within a row; in each aligned block of 96 rows (0 to 95, 96 to 191, ..., all dimensions but the last counted through in order) at most 12 rows name the same one
- w_gate_up: bfloat16 [64, 2048, 2, 1408], P('exp', None, None, 'seq'), may hold values from -0.125 to 0.125
- w_down: bfloat16 [64, 1408, 2048], P('exp', 'seq'), may hold values from -0.15625 to 0.15625
Outputs:
- layer_out: bfloat16 [32, 384, 2048], P('exp', 'seq')
Inputs may be any that keep to these rules, and one draw needn't show every extreme that they name: `expert_ids`: each point names 6 different experts. In each aligned block of 96 points (the points of one device, in the order of sets and then points), no expert is named by more than 12 points, and in every draw some expert is named by exactly 12 points of some block.
All inputs are finite; a program needn't handle non-finite values.
Results may differ from a plain program's by a relative error of at most 0.0065.
Values may be sent and summed in bfloat16 or wider, within the bound.
No kernel may reach another device: no remote copies, remote signals or barrier semaphores. Data moves between devices by JAX's collectives and lax.ppermute only.
A program may use at most 128 MiB of HBM per device.

v0:
```python
import math
import jax
import jax.numpy as jnp
from jax import lax
from jax.sharding import PartitionSpec as P

H = 16
HD = 128
EXPERTS = 64
epsilon = 1e-05


def gate_weights(normed_rows, router_w, chosen):
    logits = jnp.dot(normed_rows, router_w, preferred_element_type=jnp.float32)
    match = chosen[:, :, None] == jnp.arange(logits.shape[1], dtype=jnp.int32)[None, None, :]
    picked = jnp.sum(jnp.where(match, logits[:, None, :], jnp.zeros((), logits.dtype)), axis=-1)
    squashed = jax.nn.sigmoid(picked)
    return squashed / jnp.sum(squashed, axis=-1, keepdims=True)


def slot_ranks(chosen, block_rows, experts):
    blocks = chosen.shape[0] // block_rows
    width = block_rows * chosen.shape[1]
    grouped = chosen.reshape(blocks, width)
    hits = (grouped[:, :, None] == jnp.arange(experts, dtype=jnp.int32)[None, None, :]).astype(
        jnp.bfloat16
    )
    lower = jnp.arange(width)[:, None] >= jnp.arange(width)[None, :]
    counts = jnp.einsum(
        "ij,bje->bie", lower.astype(jnp.bfloat16), hits, preferred_element_type=jnp.float32
    )
    ranks = jnp.sum(counts * hits.astype(jnp.float32), axis=-1) - 1
    return ranks.astype(jnp.int32).reshape(chosen.shape)


def expert_part(received, w_gate_up, w_down):
    both = jnp.einsum("aend,edgf->aengf", received, w_gate_up, preferred_element_type=jnp.float32)
    hidden = (jax.nn.silu(both[:, :, :, 0]) * both[:, :, :, 1]).astype(jnp.bfloat16)
    return jnp.einsum("aenf,efd->aend", hidden, w_down, preferred_element_type=jnp.float32)


def scatter_rows(normed_rows, slot_index, buffer_rows):
    slots = jnp.arange(buffer_rows, dtype=jnp.int32)
    select = jnp.sum((slot_index[None, :, :] == slots[:, None, None]).astype(jnp.bfloat16), axis=-1)
    return jnp.dot(select, normed_rows, preferred_element_type=jnp.float32).astype(jnp.bfloat16)


def combine_rows(out_table, slot_index, gate_vals):
    slots = jnp.arange(out_table.shape[0], dtype=jnp.int32)
    weights = jnp.sum(
        jnp.where(slot_index[:, :, None] == slots[None, None, :], gate_vals[:, :, None], 0.0),
        axis=1,
    )
    high = weights.astype(jnp.bfloat16)
    low = (weights - high.astype(jnp.float32)).astype(jnp.bfloat16)
    return jnp.dot(high, out_table, preferred_element_type=jnp.float32) + jnp.dot(
        low, out_table, preferred_element_type=jnp.float32
    )


def on_device(resid, qkv, w_out, norm_gain, router_w, expert_ids, w_gate_up, w_down):
    row_count = resid.shape[1]
    model_width = resid.shape[2]
    seq_size = lax.axis_size("seq")
    exp_size = lax.axis_size("exp")
    seq_length = row_count * seq_size
    head_local = H // seq_size
    local_width = head_local * HD
    packed = qkv.reshape(row_count, 3, seq_size, local_width)
    regrouped = lax.all_to_all(packed, "seq", split_axis=2, concat_axis=0, tiled=True)
    queries = regrouped[:, 0, 0].reshape(seq_length, head_local, HD)
    keys_all = regrouped[:, 1, 0].reshape(seq_length, head_local, HD)
    values_all = regrouped[:, 2, 0].reshape(seq_length, head_local, HD)
    query_block = min(seq_length, 512)

    def attend_block(query_rows):
        scores = jnp.einsum(
            "qhd,khd->hqk", query_rows, keys_all, preferred_element_type=jnp.float32
        ) / math.sqrt(HD)
        weights = jax.nn.softmax(scores, axis=-1).astype(jnp.bfloat16)
        mixed_heads = jnp.einsum(
            "hqk,khd->qhd", weights, values_all, preferred_element_type=jnp.float32
        )
        return mixed_heads.reshape(query_rows.shape[0], local_width).astype(jnp.bfloat16)

    attended = lax.map(
        attend_block, queries.reshape(seq_length // query_block, query_block, head_local, HD)
    )
    attended = attended.reshape(seq_length, local_width)
    back = lax.all_to_all(
        attended.reshape(seq_length, 1, local_width), "seq", split_axis=0, concat_axis=1, tiled=True
    )
    point_rows = back.reshape(row_count, model_width)
    projected = jnp.dot(
        point_rows,
        lax.all_gather(w_out, "seq", axis=0, tiled=True),
        preferred_element_type=jnp.float32,
    )
    mixed = resid[0].astype(jnp.float32) + projected
    meansq = jnp.mean(mixed * mixed, axis=-1, keepdims=True)
    normed = (mixed * lax.rsqrt(meansq + epsilon) * norm_gain).astype(jnp.bfloat16)
    exp_local = w_gate_up.shape[0]
    slot_cap = row_count // 8
    gathered = lax.all_gather(normed, "seq", axis=0, tiled=True)
    chosen = expert_ids[0]
    gate_vals = gate_weights(gathered, router_w, chosen)
    ranks = slot_ranks(chosen, row_count, EXPERTS)
    owner_rows = seq_size * slot_cap
    source_block = (jnp.arange(seq_length, dtype=jnp.int32) // row_count)[:, None]
    slot_index = chosen * owner_rows + source_block * slot_cap + ranks
    outgoing = scatter_rows(gathered, slot_index, EXPERTS * owner_rows)
    outgoing = outgoing.reshape(exp_size, exp_local, owner_rows, model_width)
    partial_out = expert_part(
        lax.all_to_all(outgoing, "exp", split_axis=0, concat_axis=0, tiled=True), w_gate_up, w_down
    ).astype(jnp.bfloat16)
    returned = lax.all_to_all(partial_out, "exp", split_axis=0, concat_axis=0, tiled=True)
    out_table = returned.reshape(-1, model_width)
    expert_sum = lax.psum_scatter(
        combine_rows(out_table, slot_index, gate_vals).astype(jnp.bfloat16),
        "seq",
        scatter_dimension=0,
        tiled=True,
    ).astype(jnp.float32)
    return (mixed + expert_sum).astype(jnp.bfloat16).reshape(1, row_count, model_width)


def solution(mesh):
    in_specs = (
        P("exp", "seq", None),
        P("exp", "seq", None),
        P("seq", None),
        P(),
        P(),
        P("exp", None, None),
        P("exp", None, None, "seq"),
        P("exp", "seq", None),
    )
    out_specs = P("exp", "seq", None)
    return jax.shard_map(
        on_device, mesh=mesh, in_specs=in_specs, out_specs=out_specs, check_vma=False
    )
```

profile of v0, /device:TPU:0, one launch (start us, length us, event | category | flops | bytes accessed | tf_op | source)
XLA Modules:
  0.0 582.8 jit_solution(9345225432618470734)
XLA Ops:
  7.3 2.9 reshape.139
  11.7 27.4 %all_to_all.43 = bf16[96,3,4,512]{3,0,1,2:T(8,128)(2,1)S(1)} all-to-all(bf16[96,3,4,512]{3,0,1,2:T(8,128)(2,1)S(1)} %copy.111), channel_id=1, replica_groups=mesh['seq'=4,'exp'=32] {'seq'}, dimensions={2} | all-to-all | bytes 2359296 | tf_op jit(solution)/shard_map/all_to_all | solution.py:70
  40.2 1.9 copy.117
  42.2 1.9 copy.113
  45.0 3.5 fusion.49
  48.5 2.2 convolution_convert_fusion.1
  54.9 15.5 %all_to_all.44 = bf16[4,2,24576]{2,1,0:T(2,128)(2,1)S(1)} all-to-all(bf16[4,2,24576]{2,1,0:T(2,128)(2,1)} %reshape.149), channel_id=1, replica_groups=mesh['seq'=4,'exp'=32] {'seq'}, dimensions={0} | all-to-all | bytes 786432 | tf_op jit(solution)/shard_map/all_to_all | solution.py:90
  70.4 1.7 reshape.150
  73.7 30.5 %all-gather.3.cloned.1.call-done = bf16[2048,2048]{1,0:T(8,128)(2,1)} async-done(((bf16[512,2048]{1,0:T(8,128)(2,1)}), bf16[2048,2048]{1,0:T(8,128)(2,1)}) %all-gather.3.cloned.1.call-update) | async-done | bytes 8388624 | tf_op jit(solution)/shard_map/all_gather | solution.py:96
  104.1 5.0 multiply_reduce_fusion.1
  112.2 5.6 fusion.2
  117.8 20.6 %all-gather.5.cloned.1.call-done = bf16[384,2048]{1,0:T(8,128)(2,1)} async-done(((bf16[96,2048]{1,0:T(8,128)(2,1)}), bf16[384,2048]{1,0:T(8,128)(2,1)}) %all-gather.5.cloned.1.call-update) | async-done | bytes 1572880 | tf_op jit(solution)/shard_map/all_gather | solution.py:104
  138.4 8.7 %convolution_convert_fusion = bf16[3072,2048]{1,0:T(8,128)(2,1)S(1)} fusion(bf16[3072,384]{1,0:T(8,128)(2,1)} %fusion.2, bf16[384,2048]{1,0:T(8,128)(2,1)} %all-gather.5.cloned.1.call-done), kind=kOutput, calls=%fused_computation.9 | convolution fusion | flops 4838129664 | bytes 16515072 | tf_op jit(solution)/shard_map/dot_general | solution.py:45
  147.1 147.5 %all_to_all.45 = bf16[32,2,48,2048]{3,2,1,0:T(8,128)(2,1)} all-to-all(bf16[32,2,48,2048]{3,2,1,0:T(8,128)(2,1)S(1)} %bitcast.99), channel_id=1, replica_groups=mesh['seq'=4,'exp'=32] {'exp'}, dimensions={0} | all-to-all | bytes 25165824 | tf_op jit(solution)/shard_map/all_to_all | solution.py:114
  294.6 16.0 %fusion.8 = f32[32,2,48,2,352]{4,2,3,0,1:T(8,128)} fusion(bf16[2,2048,2,352]{1,3,2,0:T(8,128)(2,1)} %param.14, bf16[32,2,48,2048]{3,2,1,0:T(8,128)(2,1)} %all_to_all.45), kind=kOutput, calls=%fused_computation.16 | convolution fusion | flops 8858370048 | bytes 27000832 | tf_op jit(solution)/shard_map/aend,edgf->aengf/dot_general | solution.py:37
  310.6 10.7 %convert_bitcast_fusion = bf16[32,2,48,2048]{3,2,0,1:T(8,128)(2,1)S(1)} fusion(bf16[2,352,2048]{2,1,0:T(8,128)(2,1)S(1)} %copy-done, f32[32,2,48,2,352]{4,2,3,0,1:T(8,128)} %fusion.8), kind=kOutput, calls=%fused_computation.8 | convolution fusion | flops 4441964544 | bytes 24117248 | tf_op jit(solution)/shard_map/aenf,efd->aend/dot_general | solution.py:39
  321.3 5.2 copy.128
  326.5 5.2 all-to-all-start.3
  333.2 8.6 %select_reduce_fusion = f32[384,3072]{1,0:T(8,128)} fusion(f32[384,6]{0,1:T(8,128)S(1)} %multiply_divide_fusion, s32[384,6]{0,1:T(8,128)S(1)} %copy.123), kind=kLoop, calls=%fused_computation.2 | loop fusion | flops 20054016 | bytes 4737024 | tf_op jit(solution)/shard_map/reduce_sum | solution.py:50
  341.7 167.1 %all-to-all-done.3 = bf16[32,2,48,2048]{3,2,1,0:T(8,128)(2,1)} async-done(((bf16[32,2,48,2048]{3,2,1,0:T(8,128)(2,1)}), bf16[32,2,48,2048]{3,2,1,0:T(8,128)(2,1)}, u32[]{:S(2)}, u32[]{:S(2)}) %all-to-all-start.3) | async-done | bytes 12582944 | tf_op jit(solution)/shard_map/all_to_all | solution.py:116
  508.9 11.0 %fusion.32 = f32[384,2048]{1,0:T(8,128)S(1)} fusion(bf16[3072,2048]{1,0:T(8,128)(2,1)} %bitcast.26, f32[384,3072]{1,0:T(8,128)} %select_reduce_fusion), kind=kOutput, calls=%fused_computation.33 | convolution fusion | flops 4833017856 | bytes 20447232 | tf_op jit(solution)/shard_map/dot_general | solution.py:56
  519.9 9.8 %add_convert_fusion = bf16[384,2048]{1,0:T(8,128)(2,1)} fusion(f32[384,2048]{1,0:T(8,128)S(1)} %fusion.32, bf16[3072,2048]{1,0:T(8,128)(2,1)} %bitcast.26, f32[384,3072]{1,0:T(8,128)S(1)} %copy-done.3), kind=kOutput, calls=%fused_computation.17 | convolution fusion | flops 4838129664 | bytes 22020096 | tf_op jit(solution)/shard_map/dot_general | solution.py:56
  529.7 44.4 %reduce-scatter.2.cloned.1.call-done = bf16[96,2048]{1,0:T(8,128)(2,1)} async-done(((bf16[384,2048]{1,0:T(8,128)(2,1)}), bf16[96,2048]{1,0:T(8,128)(2,1)}) %reduce-scatter.2.cloned.1.call-update) | async-done | bytes 393232 | tf_op jit(solution)/shard_map/reduce_scatter | solution.py:118
  574.2 2.1 fusion.36
  (52 shorter events, 14.5 us)
Async XLA Ops:
  6.5 304.1 %copy-start = (bf16[2,352,2048]{2,1,0:T(8,128)(2,1)S(1)}, bf16[2,352,2048]{2,1,0:T(8,128)(2,1)}, u32[]{:S(2)}) copy-start(bf16[2,352,2048]{2,1,0:T(8,128)(2,1)} %param.15) | copy-start | bytes 8650756
  6.5 97.6 %all-gather.3.cloned.1.call-start = ((), (), s32[]{:S(2)}) async-start(), calls=%async_computation.5 | async-start | bytes 10485760 | tf_op jit(solution)/shard_map/all_gather | solution.py:96
  7.3 131.1 %all-gather.5.cloned.1.call-start = ((), (), s32[]{:S(2)}) async-start(), calls=%async_computation.6 | async-start | bytes 1966080 | tf_op jit(solution)/shard_map/all_gather | solution.py:104
  104.1 6.0 %copy-start.7 = (f32[2048]{0:T(1024)S(1)}, f32[2048]{0:T(1024)}, u32[]{:S(2)}) copy-start(f32[2048]{0:T(1024)} %param.11) | copy-start | bytes 24580
  104.1 6.9 %copy-start.6 = (s32[1,384,6]{1,0,2:T(1,128)S(1)}, s32[1,384,6]{1,0,2:T(1,128)}, u32[]{:S(2)}) copy-start(s32[1,384,6]{1,0,2:T(1,128)} %param.13) | copy-start | bytes 27652
  109.1 1.0 copy-start.2
  326.5 5.9 %copy-start.4 = (bf16[384,2048]{1,0:T(8,128)(2,1)S(1)}, bf16[384,2048]{1,0:T(8,128)(2,1)}, u32[]{:S(2)}) copy-start(bf16[384,2048]{1,0:T(8,128)(2,1)} %all-gather.5.cloned.1.call-done) | copy-start | bytes 4718596
  326.5 5.9 %copy-start.5 = (bf16[2048,64]{0,1:T(8,128)(2,1)S(1)}, bf16[2048,64]{0,1:T(8,128)(2,1)}, u32[]{:S(2)}) copy-start(bf16[2048,64]{0,1:T(8,128)(2,1)} %param.12) | copy-start | bytes 786436
  326.5 182.3 %all-to-all-start.3 = ((bf16[32,2,48,2048]{3,2,1,0:T(8,128)(2,1)}), bf16[32,2,48,2048]{3,2,1,0:T(8,128)(2,1)}, u32[]{:S(2)}, u32[]{:S(2)}) async-start(bf16[32,2,48,2048]{3,2,1,0:T(8,128)(2,1)} %copy.128), calls=%async_computation.3 | async-start | bytes 25165824 | tf_op jit(solution)/shard_map/all_to_all | solution.py:116
  331.7 242.5 %reduce-scatter.2.cloned.1.call-start = ((), (), s32[]{:S(2)}) async-start(), calls=%async_computation.7 | async-start | bytes 1966080 | tf_op jit(solution)/shard_map/reduce_scatter | solution.py:118
  508.9 11.0 %copy-start.3 = (f32[384,3072]{1,0:T(8,128)S(1)}, f32[384,3072]{1,0:T(8,128)}, u32[]{:S(2)}) copy-start(f32[384,3072]{1,0:T(8,128)} %select_reduce_fusion) | copy-start | bytes 14155780
  519.9 56.3 %copy-start.1 = (bf16[2,352,2048]{2,1,0:T(8,128)(2,1)S(1)}, bf16[2,352,2048]{2,1,0:T(8,128)(2,1)}, u32[]{:S(2)}) copy-start(bf16[2,352,2048]{2,1,0:T(8,128)(2,1)} %param.15) | copy-start | bytes 8650756
Sparse Core Ops, SparseCore 0:
  9.0 95.0 all-gather.2
  111.1 27.2 all-gather.4
  529.9 44.2 reduce-scatter.1
where the time goes:
time: 583 us
  waiting for transfers between devices  263 us (45%)
  blocking collectives  190 us (33%)
  matrix products  68 us (12%)
  local copies, waits for them, and re-layouts  23.2 us (4%)
  other arithmetic  18.9 us (3%)
  between operations  13.3 us (2%)
    all_to_all x1, waiting for transfers between devices, on_device(): lax.all_to_all(partial_out, 'exp', split_axis=0, concat_axis=0, tiled=True)  167 us
    all_to_all x1, blocking collectives, on_device(): lax.all_to_all(outgoing, 'exp', split_axis=0, concat_axis=0, tiled=True)  148 us
    reduce_scatter x1, waiting for transfers between devices, on_device(): lax.psum_scatter(combine_rows(out_table, slot_index, gate_vals).astype(jn...  44.4 us
    all_gather x1, waiting for transfers between devices, on_device(): lax.all_gather(w_out, 'seq', axis=0, tiled=True)  30.5 us
    all_to_all x1, blocking collectives, on_device(): lax.all_to_all(packed, 'seq', split_axis=2, concat_axis=0, tiled=True)  27.4 us
    all_gather x1, waiting for transfers between devices, on_device(): gathered = lax.all_gather(normed, 'seq', axis=0, tiled=True)  20.6 us
    dot_general x1, matrix products, expert_part(): jnp.einsum('aend,edgf->aengf', received, w_gate_up, preferred_element_typ...  16 us
    all_to_all x1, blocking collectives, on_device(): lax.all_to_all(attended.reshape(seq_length, 1, local_width), 'seq', split...  15.5 us
  transfers between devices with their start and end apart: 4, of which 4 were waited for; matrix products, arithmetic and copies ran while one was open for 7% of the time, Pallas kernels for 0%

commit v1 on v0

--- a/solution.py
+++ b/solution.py
@@ -93,7 +93,9 @@
     point_rows = back.reshape(row_count, model_width)
     projected = jnp.dot(
         point_rows,
-        lax.all_gather(w_out, "seq", axis=0, tiled=True),
+        jnp.concatenate(
+            lax.all_to_all(jnp.stack([w_out] * lax.axis_size("seq")), "seq", 0, 0), axis=0
+        ),
         preferred_element_type=jnp.float32,
     )
     mixed = resid[0].astype(jnp.float32) + projected

time: 583 us -> 641 us (1.099)
  waiting for transfers between devices: 263 us -> 320 us
  blocking collectives: 190 us -> 179 us
    all_to_all x0 -> x1, waiting for transfers between devices: none -> 88.3 us  [on_device(): lax.all_to_all(jnp.stack([w_out] * lax.axis_size('seq')), 'seq', 0, 0)]
    all_gather x1 -> x0, waiting for transfers between devices: 30.5 us -> none  [on_device(): lax.all_gather(w_out, 'seq', axis=0, tiled=True)]
    all_to_all x1, blocking collectives: 27.4 us -> 20.7 us  [on_device(): lax.all_to_all(packed, 'seq', split_axis=2, concat_axis=0, tiled=True)]
  transfers between devices with their start and end apart: 4 -> 4, of which waited for: 4 -> 4; matrix products, arithmetic and copies ran while one was open for 7% -> 3% of each run, Pallas kernels for 0% -> 0%
where the time goes in v1:
time: 641 us; the launch traced here: 640 us
  waiting for transfers between devices  320 us (50%)
  blocking collectives  179 us (28%)
  matrix products  68 us (11%)
  local copies, waits for them, and re-layouts  29.1 us (5%)
  other arithmetic  19 us (3%)
  between operations  13.6 us (2%)
  starting transfers between devices  11.4 us (2%)
    all_to_all x1, waiting for transfers between devices, on_device(): lax.all_to_all(partial_out, 'exp', split_axis=0, concat_axis=0, tiled=True)  167 us
    all_to_all x1, blocking collectives, on_device(): lax.all_to_all(outgoing, 'exp', split_axis=0, concat_axis=0, tiled=True)  148 us
    all_to_all x1, waiting for transfers between devices, on_device(): lax.all_to_all(jnp.stack([w_out] * lax.axis_size('seq')), 'seq', 0, 0)  88.3 us
    reduce_scatter x1, waiting for transfers between devices, on_device(): lax.psum_scatter(combine_rows(out_table, slot_index, gate_vals).astype(jn...  44.4 us
    all_to_all x1, blocking collectives, on_device(): lax.all_to_all(packed, 'seq', split_axis=2, concat_axis=0, tiled=True)  20.7 us
    all_gather x1, waiting for transfers between devices, on_device(): gathered = lax.all_gather(normed, 'seq', axis=0, tiled=True)  20.3 us
    dot_general x1, matrix products, expert_part(): jnp.einsum('aend,edgf->aengf', received, w_gate_up, preferred_element_typ...  16 us
  transfers between devices with their start and end apart: 4, of which 4 were waited for; matrix products, arithmetic and copies ran while one was open for 3% of the time, Pallas kernels for 0%

profile of v1, /device:TPU:0, one launch (start us, length us, event | category | flops | bytes accessed | tf_op | source)
XLA Modules:
  0.0 640.3 jit_solution(17354034315942806847)
XLA Ops:
  6.5 2.9 reshape.144
  11.0 20.7 %all_to_all.48 = bf16[96,3,4,512]{3,0,1,2:T(8,128)(2,1)S(1)} all-to-all(bf16[96,3,4,512]{3,0,1,2:T(8,128)(2,1)S(1)} %copy.111), channel_id=1, replica_groups=mesh['seq'=4,'exp'=32] {'seq'}, dimensions={2} | all-to-all | bytes 2359296 | tf_op jit(solution)/shard_map/all_to_all | solution.py:70
  34.6 1.9 copy.113
  37.5 3.4 fusion.49
  40.8 2.2 convolution_convert_fusion.1
  47.5 10.8 %all_to_all.49 = bf16[4,2,24576]{2,1,0:T(2,128)(2,1)S(1)} all-to-all(bf16[4,2,24576]{2,1,0:T(2,128)(2,1)} %reshape.155), channel_id=1, replica_groups=mesh['seq'=4,'exp'=32] {'seq'}, dimensions={0} | all-to-all | bytes 786432 | tf_op jit(solution)/shard_map/all_to_all | solution.py:90
  58.3 5.9 stack.2
  64.2 5.7 all-to-all-start.2
  73.3 88.3 %all-to-all-done.2 = bf16[4,512,2048]{2,1,0:T(8,128)(2,1)} async-done(((bf16[4,512,2048]{2,1,0:T(8,128)(2,1)}), bf16[4,512,2048]{2,1,0:T(8,128)(2,1)}, u32[]{:S(2)}, u32[]{:S(2)}) %all-to-all-start.2) | async-done | bytes 8388640 | tf_op jit(solution)/shard_map/all_to_all | solution.py:97
  161.7 5.0 multiply_reduce_fusion.1
  169.7 5.6 fusion.2
  175.3 20.3 %all-gather.2.cloned.1.call-done = bf16[384,2048]{1,0:T(8,128)(2,1)} async-done(((bf16[96,2048]{1,0:T(8,128)(2,1)}), bf16[384,2048]{1,0:T(8,128)(2,1)}) %all-gather.2.cloned.1.call-update) | async-done | bytes 1572880 | tf_op jit(solution)/shard_map/all_gather | solution.py:106
  195.6 8.7 %convolution_convert_fusion = bf16[3072,2048]{1,0:T(8,128)(2,1)S(1)} fusion(bf16[3072,384]{1,0:T(8,128)(2,1)} %fusion.2, bf16[384,2048]{1,0:T(8,128)(2,1)} %all-gather.2.cloned.1.call-done), kind=kOutput, calls=%fused_computation.9 | convolution fusion | flops 4838129664 | bytes 16515072 | tf_op jit(solution)/shard_map/dot_general | solution.py:45
  204.3 147.5 %all_to_all.50 = bf16[32,2,48,2048]{3,2,1,0:T(8,128)(2,1)} all-to-all(bf16[32,2,48,2048]{3,2,1,0:T(8,128)(2,1)S(1)} %bitcast.100), channel_id=1, replica_groups=mesh['seq'=4,'exp'=32] {'exp'}, dimensions={0} | all-to-all | bytes 25165824 | tf_op jit(solution)/shard_map/all_to_all | solution.py:116
  351.8 16.0 %fusion.8 = f32[32,2,48,2,352]{4,2,3,0,1:T(8,128)} fusion(bf16[2,2048,2,352]{1,3,2,0:T(8,128)(2,1)} %param.14, bf16[32,2,48,2048]{3,2,1,0:T(8,128)(2,1)} %all_to_all.50), kind=kOutput, calls=%fused_computation.16 | convolution fusion | flops 8858370048 | bytes 27000832 | tf_op jit(solution)/shard_map/aend,edgf->aengf/dot_general | solution.py:37
  367.8 10.7 %convert_bitcast_fusion = bf16[32,2,48,2048]{3,2,0,1:T(8,128)(2,1)S(1)} fusion(bf16[2,352,2048]{2,1,0:T(8,128)(2,1)S(1)} %copy-done, f32[32,2,48,2,352]{4,2,3,0,1:T(8,128)} %fusion.8), kind=kOutput, calls=%fused_computation.8 | convolution fusion | flops 4441964544 | bytes 24117248 | tf_op jit(solution)/shard_map/aenf,efd->aend/dot_general | solution.py:39
  378.6 5.2 copy.128
  383.8 5.2 all-to-all-start.4
  390.4 8.6 %select_reduce_fusion = f32[384,3072]{1,0:T(8,128)} fusion(f32[384,6]{0,1:T(8,128)S(1)} %multiply_divide_fusion, s32[384,6]{0,1:T(8,128)S(1)} %copy.123), kind=kLoop, calls=%fused_computation.2 | loop fusion | flops 20054016 | bytes 4737024 | tf_op jit(solution)/shard_map/reduce_sum | solution.py:50
  399.0 167.1 %all-to-all-done.4 = bf16[32,2,48,2048]{3,2,1,0:T(8,128)(2,1)} async-done(((bf16[32,2,48,2048]{3,2,1,0:T(8,128)(2,1)}), bf16[32,2,48,2048]{3,2,1,0:T(8,128)(2,1)}, u32[]{:S(2)}, u32[]{:S(2)}) %all-to-all-start.4) | async-done | bytes 12582944 | tf_op jit(solution)/shard_map/all_to_all | solution.py:118
  566.1 11.0 %fusion.32 = f32[384,2048]{1,0:T(8,128)S(1)} fusion(bf16[3072,2048]{1,0:T(8,128)(2,1)} %bitcast.27, f32[384,3072]{1,0:T(8,128)} %select_reduce_fusion), kind=kOutput, calls=%fused_computation.33 | convolution fusion | flops 4833017856 | bytes 20447232 | tf_op jit(solution)/shard_map/dot_general | solution.py:56
  577.2 9.8 %add_convert_fusion = bf16[384,2048]{1,0:T(8,128)(2,1)} fusion(f32[384,2048]{1,0:T(8,128)S(1)} %fusion.32, bf16[3072,2048]{1,0:T(8,128)(2,1)} %bitcast.27, f32[384,3072]{1,0:T(8,128)S(1)} %copy-done.3), kind=kOutput, calls=%fused_computation.17 | convolution fusion | flops 4838129664 | bytes 22020096 | tf_op jit(solution)/shard_map/dot_general | solution.py:56
  587.0 44.4 %reduce-scatter.2.cloned.1.call-done = bf16[96,2048]{1,0:T(8,128)(2,1)} async-done(((bf16[384,2048]{1,0:T(8,128)(2,1)}), bf16[96,2048]{1,0:T(8,128)(2,1)}) %reduce-scatter.2.cloned.1.call-update) | async-done | bytes 393232 | tf_op jit(solution)/shard_map/reduce_scatter | solution.py:120
  631.4 2.1 fusion.36
  (52 shorter events, 17.7 us)
Async XLA Ops:
  6.5 361.3 %copy-start = (bf16[2,352,2048]{2,1,0:T(8,128)(2,1)S(1)}, bf16[2,352,2048]{2,1,0:T(8,128)(2,1)}, u32[]{:S(2)}) copy-start(bf16[2,352,2048]{2,1,0:T(8,128)(2,1)} %param.15) | copy-start | bytes 8650756
  64.2 97.5 %all-to-all-start.2 = ((bf16[4,512,2048]{2,1,0:T(8,128)(2,1)}), bf16[4,512,2048]{2,1,0:T(8,128)(2,1)}, u32[]{:S(2)}, u32[]{:S(2)}) async-start(bf16[4,512,2048]{2,1,0:T(8,128)(2,1)} %stack.2), calls=%async_computation.2 | async-start | bytes 16777216 | tf_op jit(solution)/shard_map/all_to_all | solution.py:97
  69.9 125.8 %all-gather.2.cloned.1.call-start = ((), (), s32[]{:S(2)}) async-start(), calls=%async_computation.6 | async-start | bytes 1966080 | tf_op jit(solution)/shard_map/all_gather | solution.py:106
  161.7 6.0 copy-start.7
  161.7 6.9 %copy-start.6 = (s32[1,384,6]{1,0,2:T(1,128)S(1)}, s32[1,384,6]{1,0,2:T(1,128)}, u32[]{:S(2)}) copy-start(s32[1,384,6]{1,0,2:T(1,128)} %param.13) | copy-start | bytes 27652
  166.7 0.9 copy-start.2
  383.8 5.9 copy-start.4
  383.8 5.9 copy-start.5
  383.8 182.3 %all-to-all-start.4 = ((bf16[32,2,48,2048]{3,2,1,0:T(8,128)(2,1)}), bf16[32,2,48,2048]{3,2,1,0:T(8,128)(2,1)}, u32[]{:S(2)}, u32[]{:S(2)}) async-start(bf16[32,2,48,2048]{3,2,1,0:T(8,128)(2,1)} %copy.128), calls=%async_computation.4 | async-start | bytes 25165824 | tf_op jit(solution)/shard_map/all_to_all | solution.py:118
  389.0 242.5 %reduce-scatter.2.cloned.1.call-start = ((), (), s32[]{:S(2)}) async-start(), calls=%async_computation.7 | async-start | bytes 1966080 | tf_op jit(solution)/shard_map/reduce_scatter | solution.py:120
  566.1 11.0 %copy-start.3 = (f32[384,3072]{1,0:T(8,128)S(1)}, f32[384,3072]{1,0:T(8,128)}, u32[]{:S(2)}) copy-start(f32[384,3072]{1,0:T(8,128)} %select_reduce_fusion) | copy-start | bytes 14155780
  577.2 56.3 %copy-start.1 = (bf16[2,352,2048]{2,1,0:T(8,128)(2,1)S(1)}, bf16[2,352,2048]{2,1,0:T(8,128)(2,1)}, u32[]{:S(2)}) copy-start(bf16[2,352,2048]{2,1,0:T(8,128)(2,1)} %param.15) | copy-start | bytes 8650756
Sparse Core Ops, SparseCore 0:
  168.6 26.9 all-gather.1
  587.1 44.2 reduce-scatter.1
